TPU v7x, 256 devices: a whole 4x4x8 slice. The times are simulated.
256 devices in a mesh: row: 16 (over x, y), ka: 16 (over z, core).
Axes of the slice: x: 4, y: 4, z: 8, core: 2. Of those that a mesh axis runs over, the one named last changes fastest.
Arguments:
- t2: bfloat16 [16, 4096, 128], P('row', 'ka'), may hold values from -6 to 6
- vtiles: bfloat16 [16, 16, 160, 128, 128], P('row', 'ka'), may hold values from -0.078125 to 0.078125
- need_cd: int32 [16, 16, 64], P(None, 'ka'), may hold values from 0 to 255, as said below
- tile_cd: int32 [16, 16, 160], P('row', 'ka'), may hold values from 0 to 63
- tile_ab: int32 [16, 16, 160], P('row', 'ka'), may hold values from 0 to 63
Outputs:
- ladder: bfloat16 [1024, 16, 128], P(('row', 'ka'))
Inputs may be any that keep to these rules, and one draw needn't show every extreme that they name: `need_cd`: the 64 entries of one block's list are all different.
All inputs are finite; a program needn't handle non-finite values.
Results may differ from a plain program's by a relative error of at most 0.0015.
Values may be sent and summed in bfloat16 or wider, within the bound.
No kernel may reach another device: no remote copies, remote signals or barrier semaphores. Data moves between devices by JAX's collectives and lax.ppermute only.
A program may use at most 64 MiB of HBM per device.

v0:
```python
import jax
import jax.numpy as jnp
from jax import lax
from jax.sharding import PartitionSpec as P

AB_DEV = 64


def on_device(t2, vtiles, need_cd, tile_cd, tile_ab):
    pairs_all = t2.shape[0] * lax.axis_size("row")
    tile_edge = t2.shape[2]
    slot_cd = tile_cd[0, 0]
    slot_ab = tile_ab[0, 0]
    blocks = vtiles[0, 0]
    slot_count = slot_cd.shape[0]
    own_list = lax.dynamic_index_in_dim(need_cd[:, 0, :], lax.axis_index("row"), 0, keepdims=False)
    whole = lax.all_gather(t2, "row", axis=0, tiled=True)
    picked = jnp.take(whole, own_list[slot_cd], axis=1)
    products = jnp.einsum("pst,stu->spu", picked, blocks, preferred_element_type=jnp.float32)
    products = products.reshape(slot_count, pairs_all * tile_edge)
    upper_part = lax.optimization_barrier(products.astype(jnp.bfloat16))
    lower_part = (products - upper_part.astype(jnp.float32)).astype(jnp.bfloat16)
    share = AB_DEV // lax.axis_size("ka")
    wanted_rows = lax.iota(jnp.int32, share * lax.axis_size("ka"))
    onehot = (slot_ab[None, :] == wanted_rows[:, None]).astype(jnp.bfloat16)
    summed = jnp.dot(onehot, upper_part, preferred_element_type=jnp.float32)
    summed = summed + jnp.dot(onehot, lower_part, preferred_element_type=jnp.float32)
    reduced = lax.psum_scatter(
        summed.reshape(share * lax.axis_size("ka"), pairs_all, tile_edge),
        "ka",
        scatter_dimension=0,
        tiled=True,
    )
    return reduced.astype(jnp.bfloat16)


def solution(mesh):
    return jax.shard_map(
        on_device,
        mesh=mesh,
        in_specs=(
            P("row", "ka", None),
            P("row", "ka", None, None, None),
            P(None, "ka", None),
            P("row", "ka", None),
            P("row", "ka", None),
        ),
        out_specs=P(("row", "ka"), None, None),
        check_vma=False,
    )
```

profile of v0, /device:TPU:6, one launch (start us, length us, event | category | flops | bytes accessed | tf_op | source)
XLA Modules:
  0.0 133.9 jit_solution(1743452980378425177)
XLA Ops:
  6.5 0.0 copy-start
  6.5 0.0 all-gather.2.cloned.1.call-start
  6.5 0.7 all-gather.2.cloned.1.call-update
  7.3 0.0 reduce-scatter.2.cloned.1.call-start
  7.3 0.0 copy-done
  7.3 0.7 compare_select_fusion.1
  8.0 1.5 %gather_fusion = s32[160]{0:T(256)S(1)} fusion(s32[64]{0:T(128)S(1)} %dynamic-slice_bitcast_fusion, s32[1024]{0:T(1024)S(1)} %pad_clamp_fusion.1), kind=kCustom, calls=%fused_computation | custom fusion | bytes 1920 | tf_op jit(solution)/shard_map/gather | solution.py:18
  9.6 50.2 %all-gather.2.cloned.1.call-done = bf16[16,256,128]{2,1,0:T(8,128)(2,1)} async-done(((bf16[1,256,128]{2,1,0:T(8,128)(2,1)}), bf16[16,256,128]{2,1,0:T(8,128)(2,1)}) %all-gather.2.cloned.1.call-update) | async-done | bytes 1048592 | tf_op jit(solution)/shard_map/all_gather | solution.py:17
  59.8 1.9 %copy.8 = bf16[16,256,128]{2,0,1:T(8,128)(2,1)S(1)} copy(bf16[16,256,128]{2,1,0:T(8,128)(2,1)} %all-gather.2.cloned.1.call-done) | data formatting | bytes 2097152 | tf_op jit(solution)/shard_map/all_gather | solution.py:17
  61.7 0.7 gather_fusion.1
  62.5 3.5 %fusion = f32[160,16,128]{2,1,0:T(8,128)S(1)} fusion(bf16[1,1,160,128,128]{4,3,2,1,0:T(8,128)(2,1)} %param.6, bf16[160,16,128]{2,1,0:T(8,128)(2,1)S(1)} %gather_fusion.1, pred[160]{0:T(512)(128)(4,1)S(1)} %compare_and_fusion), kind=kOutput, calls=%fused_computation.2 | convolution fusion | flops 84213760 | bytes 7209120 | tf_op jit(solution)/shard_map/pst,stu->spu/dot_general | solution.py:19
  66.0 0.0 copy-start.1
  66.0 0.5 copy.14
  66.5 0.2 copy-done.1
  66.7 0.2 fusion.9
  66.9 0.6 fusion.3
  67.5 0.9 copy.10
  68.3 0.0 reduce-scatter.2.cloned.1.call-update
  68.4 57.3 %reduce-scatter.2.cloned.1.call-done = f32[4,16,128]{2,1,0:T(8,128)} async-done(((f32[64,16,128]{2,1,0:T(8,128)}), f32[4,16,128]{2,1,0:T(8,128)}) %reduce-scatter.2.cloned.1.call-update) | async-done | bytes 32784 | tf_op jit(solution)/shard_map/reduce_scatter | solution.py:28
  125.6 1.4 %convert_element_type.16 = bf16[4,16,128]{2,1,0:T(8,128)(2,1)} convert(f32[4,16,128]{2,1,0:T(8,128)} %reduce-scatter.2.cloned.1.call-done) | non-fusion elementwise | flops 8192 | bytes 49152 | tf_op jit(solution)/shard_map/convert_element_type | solution.py:34
  (5 shorter events, 0.0 us)
Async XLA Ops:
  6.5 0.8 copy-start
  6.5 53.3 %all-gather.2.cloned.1.call-start = ((), (), s32[]{:S(2)}) async-start(), calls=%async_computation.1 | async-start | bytes 1114112 | tf_op jit(solution)/shard_map/all_gather | solution.py:17
  7.3 118.4 %reduce-scatter.2.cloned.1.call-start = ((), (), s32[]{:S(2)}) async-start(), calls=%async_computation.2 | async-start | bytes 557056 | tf_op jit(solution)/shard_map/reduce_scatter | solution.py:28
  66.0 0.7 copy-start.1
Sparse Core Ops, SparseCore 0:
  9.8 50.0 all-gather.1
  68.5 57.1 reduce-scatter.1
where the time goes:
time: 134 us
  waiting for transfers between devices  108 us (81%)
  between operations  13.5 us (10%)
  local copies, waits for them, and re-layouts  5.76 us (4%)
  matrix products  4.26 us (3%)
  other arithmetic  2.08 us (2%)
    reduce_scatter x1, waiting for transfers between devices, on_device(): lax.psum_scatter(summed.reshape(share * lax.axis_size('ka'), pairs_all, t...  57.3 us
    all_gather x1, waiting for transfers between devices, on_device(): whole = lax.all_gather(t2, 'row', axis=0, tiled=True)  50.2 us
    dot_general x1, matrix products, on_device(): jnp.einsum('pst,stu->spu', picked, blocks, preferred_element_type=jnp.flo...  3.47 us
  transfers between devices with their start and end apart: 2, of which 2 were waited for; matrix products, arithmetic and copies ran while one was open for 2% of the time, Pallas kernels for 0%

commit v1 on v0

--- a/solution.py
+++ b/solution.py
@@ -14,7 +14,15 @@
     blocks = vtiles[0, 0]
     slot_count = slot_cd.shape[0]
     own_list = lax.dynamic_index_in_dim(need_cd[:, 0, :], lax.axis_index("row"), 0, keepdims=False)
-    whole = lax.all_gather(t2, "row", axis=0, tiled=True)
+    whole = jnp.concatenate(
+        lax.all_to_all(
+            jnp.stack(lax.axis_size("row") * [t2], axis=0),
+            concat_axis=0,
+            split_axis=0,
+            axis_name="row",
+        ),
+        axis=0,
+    )
     picked = jnp.take(whole, own_list[slot_cd], axis=1)
     products = jnp.einsum("pst,stu->spu", picked, blocks, preferred_element_type=jnp.float32)
     products = products.reshape(slot_count, pairs_all * tile_edge)

time: 134 us -> 106 us (0.79)
  waiting for transfers between devices: 108 us -> 72.3 us
  starting transfers between devices: 0.04 us -> 7.59 us
    all_gather x1 -> x0, waiting for transfers between devices: 50.2 us -> none  [on_device(): whole = lax.all_gather(t2, 'row', axis=0, tiled=True)]
    all_to_all x0 -> x1, waiting for transfers between devices: none -> 13.5 us  [on_device(): lax.all_to_all(jnp.stack(lax.axis_size('row') * [t2], axis=0), concat_axi...]
    all_to_all x0 -> x1, starting transfers between devices: none -> 7.56 us  [on_device(): lax.all_to_all(jnp.stack(lax.axis_size('row') * [t2], axis=0), concat_axi...]
    another operation x0 -> x1, local copies, waits for them, and re-layouts: none -> 2.03 us  [on_device(): jnp.stack(lax.axis_size('row') * [t2], axis=0)]
    all_gather x1 -> x0, local copies, waits for them, and re-layouts: 1.9 us -> none  [on_device(): whole = lax.all_gather(t2, 'row', axis=0, tiled=True)]
    reduce_scatter x1, waiting for transfers between devices: 57.3 us -> 58.8 us  [on_device(): lax.psum_scatter(summed.reshape(share * lax.axis_size('ka'), pairs_all, t...]
where the time goes in v1:
time: 106 us
  waiting for transfers between devices  72.3 us (68%)
  between operations  13.5 us (13%)
  starting transfers between devices  7.59 us (7%)
  local copies, waits for them, and re-layouts  6.57 us (6%)
  matrix products  4.27 us (4%)
  other arithmetic  1.39 us (1%)
    reduce_scatter x1, waiting for transfers between devices, on_device(): lax.psum_scatter(summed.reshape(share * lax.axis_size('ka'), pairs_all, t...  58.8 us
    all_to_all x1, waiting for transfers between devices, on_device(): lax.all_to_all(jnp.stack(lax.axis_size('row') * [t2], axis=0), concat_axi...  13.5 us
    all_to_all x1, starting transfers between devices, on_device(): lax.all_to_all(jnp.stack(lax.axis_size('row') * [t2], axis=0), concat_axi...  7.56 us
    dot_general x1, matrix products, on_device(): jnp.einsum('pst,stu->spu', picked, blocks, preferred_element_type=jnp.flo...  3.47 us
    gather x2, local copies, waits for them, and re-layouts, on_device(): picked = jnp.take(whole, own_list[slot_cd], axis=1)  2.3 us
  transfers between devices with their start and end apart: 2, of which 2 were waited for; matrix products, arithmetic and copies ran while one was open for 2% of the time, Pallas kernels for 0%

profile of v1, /device:TPU:6, one launch (start us, length us, event | category | flops | bytes accessed | tf_op | source)
XLA Modules:
  0.0 105.7 jit_solution(17192712103504274295)
XLA Ops:
  6.5 0.0 copy-start
  6.5 2.0 %stack.2 = bf16[16,1,256,128]{3,2,1,0:T(8,128)(2,1)} broadcast(bf16[256,128]{1,0:T(8,128)(2,1)} %bitcast.36), dimensions={2,3} | broadcast | bytes 1114112 | tf_op jit(solution)/shard_map/stack | solution.py:19
  8.6 0.0 copy-start.2
  8.6 7.6 %all-to-all-start = ((bf16[16,1,256,128]{3,2,1,0:T(8,128)(2,1)}), bf16[16,1,256,128]{3,2,1,0:T(8,128)(2,1)S(1)}, u32[]{:S(2)}, u32[]{:S(2)}) async-start(bf16[16,1,256,128]{3,2,1,0:T(8,128)(2,1)} %stack.2), calls=%async_computation | async-start | bytes 2097152 | tf_op jit(solution)/shard_map/all_to_all | solution.py:18
  16.1 0.0 reduce-scatter.2.cloned.1.call-start
  16.2 0.0 copy-done
  16.2 0.0 copy-done.2
  16.2 1.6 %gather_fusion = s32[160]{0:T(256)S(1)} fusion(s32[64]{0:T(128)S(1)} %dynamic-slice_bitcast_fusion, s32[1024]{0:T(1024)S(1)} %pad_clamp_fusion.1), kind=kCustom, calls=%fused_computation | custom fusion | bytes 1920 | tf_op jit(solution)/shard_map/gather | solution.py:26
  17.8 13.5 %all-to-all-done = bf16[16,1,256,128]{3,2,1,0:T(8,128)(2,1)S(1)} async-done(((bf16[16,1,256,128]{3,2,1,0:T(8,128)(2,1)}), bf16[16,1,256,128]{3,2,1,0:T(8,128)(2,1)S(1)}, u32[]{:S(2)}, u32[]{:S(2)}) %all-to-all-start) | async-done | bytes 1048608 | tf_op jit(solution)/shard_map/all_to_all | solution.py:18
  31.4 0.7 copy.14
  32.0 0.7 gather_fusion.1
  32.8 3.5 %fusion = f32[160,16,128]{2,1,0:T(8,128)S(1)} fusion(bf16[1,1,160,128,128]{4,3,2,1,0:T(8,128)(2,1)} %param.6, bf16[160,16,128]{2,1,0:T(8,128)(2,1)S(1)} %gather_fusion.1, pred[160]{0:T(512)(128)(4,1)S(1)} %compare_and_fusion), kind=kOutput, calls=%fused_computation.2 | convolution fusion | flops 84213760 | bytes 7209120 | tf_op jit(solution)/shard_map/pst,stu->spu/dot_general | solution.py:27
  36.3 0.0 copy-start.1
  36.3 0.5 copy.13
  36.8 0.2 copy-done.1
  36.9 0.2 fusion.9
  37.2 0.6 fusion.3
  37.8 0.9 copy.8
  38.6 0.0 reduce-scatter.2.cloned.1.call-update
  38.7 58.8 %reduce-scatter.2.cloned.1.call-done = f32[4,16,128]{2,1,0:T(8,128)} async-done(((f32[64,16,128]{2,1,0:T(8,128)}), f32[4,16,128]{2,1,0:T(8,128)}) %reduce-scatter.2.cloned.1.call-update) | async-done | bytes 32784 | tf_op jit(solution)/shard_map/reduce_scatter | solution.py:36
  97.5 1.4 %convert_element_type.16 = bf16[4,16,128]{2,1,0:T(8,128)(2,1)} convert(f32[4,16,128]{2,1,0:T(8,128)} %reduce-scatter.2.cloned.1.call-done) | non-fusion elementwise | flops 8192 | bytes 49152 | tf_op jit(solution)/shard_map/convert_element_type | solution.py:42
  (6 shorter events, 0.0 us)
Async XLA Ops:
  6.5 9.6 %copy-start = (s32[16,1,64]{2,1,0:T(1,128)S(1)}, s32[16,1,64]{2,1,0:T(1,128)}, u32[]{:S(2)}) copy-start(s32[16,1,64]{2,1,0:T(1,128)} %param.7) | copy-start | bytes 12292
  8.6 7.6 %copy-start.2 = (s32[1,1,160]{2,1,0:T(1,128)S(1)}, s32[1,1,160]{2,1,0:T(1,128)}, u32[]{:S(2)}) copy-start(s32[1,1,160]{2,1,0:T(1,128)} %param.8) | copy-start | bytes 1924
  8.6 22.8 %all-to-all-start = ((bf16[16,1,256,128]{3,2,1,0:T(8,128)(2,1)}), bf16[16,1,256,128]{3,2,1,0:T(8,128)(2,1)S(1)}, u32[]{:S(2)}, u32[]{:S(2)}) async-start(bf16[16,1,256,128]{3,2,1,0:T(8,128)(2,1)} %stack.2), calls=%async_computation | async-start | bytes 2097152 | tf_op jit(solution)/shard_map/all_to_all | solution.py:18
  16.1 81.3 %reduce-scatter.2.cloned.1.call-start = ((), (), s32[]{:S(2)}) async-start(), calls=%async_computation.2 | async-start | bytes 557056 | tf_op jit(solution)/shard_map/reduce_scatter | solution.py:36
  36.3 0.7 copy-start.1
Sparse Core Ops, SparseCore 0:
  38.8 58.6 reduce-scatter.1
